TPU v7x, 128 devices: a whole 4x4x4 slice. The times are simulated.
128 devices in a mesh: az: 16 (over z, y), rg: 8 (over x, core).
Axes of the slice: x: 4, y: 4, z: 4, core: 2. Of those that a mesh axis runs over, the one named last changes fastest.
Arguments:
- master_phasor_raster: bfloat16 [2, 2560, 10240], P(None, ('az', 'rg')), may hold values from -6 to 6
- slave_phasor_raster: bfloat16 [2, 2560, 10240], P(None, ('az', 'rg')), may hold values from -6 to 6
- segment_track_trim: int32 [16, 2], replicated, may hold values from 0 to 16
- segment_slant_trim: int32 [16, 2], replicated, may hold values from 0 to 96
Outputs:
- phase: float32 [512, 2048], P('az', 'rg')
- weight: float32 [512, 2048], P('az', 'rg')
Inputs may be any that keep to these rules, and one draw needn't show every extreme that they name: segment_track_trim rows hold invalid line counts at the start and end of each burst. segment_slant_trim rows hold invalid column counts at the near and far range edge of each burst.
All inputs are finite; a program needn't handle non-finite values.
Results may differ from a plain program's by a relative error of at most 0.0003.
Values may be sent and summed in bfloat16 or wider, within the bound.
No kernel may reach another device: no remote copies, remote signals or barrier semaphores. Data moves between devices by JAX's collectives and lax.ppermute only.
A program may use at most 128 MiB of HBM per device.

v0:
```python
import jax
import jax.numpy as jnp
from jax import lax
from jax.sharding import PartitionSpec as P

LOOK = 5
LEVELS = 6
ITERS = 3
SWEEPS = 4
SEGMENT_HEIGHT = 160
COLS_DEV = 1280


OMEGA = 0.6
MU = 0.01


def extended(cells, sides, width):
    for axis, dim in sides:
        count = lax.axis_size(axis)
        ends = count - 1
        head = lax.slice_in_dim(cells, 0, width, axis=dim)
        tail = lax.slice_in_dim(cells, cells.shape[dim] - width, cells.shape[dim], axis=dim)
        cells = jnp.concatenate(
            [
                lax.ppermute(tail, axis, [(i, (i + 1) % count) for i in range(ends)]),
                cells,
                lax.ppermute(head, axis, [((i + 1) % count, i) for i in range(ends)]),
            ],
            axis=dim,
        )
    return cells


def mean_multilook(
    leading_phasor_raster,
    trailing_phasor_raster,
    along_track_position,
    column_index,
    track_trim_width,
    slant_trim_width,
    slant_sample_total,
):
    usable_stripes = (along_track_position >= track_trim_width[0]) & (
        along_track_position < SEGMENT_HEIGHT - track_trim_width[1]
    )
    cols_ok = (column_index >= slant_trim_width[0]) & (
        column_index < slant_sample_total - slant_trim_width[1]
    )
    valid_mask = (usable_stripes[:, None] & cols_ok[None, :]).astype(jnp.float32)
    first_re = leading_phasor_raster[0].astype(jnp.float32) * valid_mask
    first_im = leading_phasor_raster[1].astype(jnp.float32) * valid_mask
    second_re = trailing_phasor_raster[0].astype(jnp.float32) * valid_mask
    second_im = trailing_phasor_raster[1].astype(jnp.float32) * valid_mask
    products = jnp.stack(
        [
            first_re * second_re + first_im * second_im,
            first_im * second_re - first_re * second_im,
            first_re * first_re + first_im * first_im,
            second_re * second_re + second_im * second_im,
        ]
    )
    height_rows, width_cols = valid_mask.shape
    return products.reshape(4, height_rows // LOOK, LOOK, width_cols // LOOK, LOOK).sum(axis=(2, 4))


def edge_terms(left_re, left_im, left_weight, right_re, right_im, right_weight):
    edge_weight = 0.5 * (left_weight + right_weight)
    cross_im = right_im * left_re - right_re * left_im
    power_sum = (
        left_re * left_re + left_im * left_im + right_re * right_re + right_im * right_im + 1.0
    )
    return (edge_weight, 2.0 * cross_im / power_sum)


def combine_padded(vector, padded, operators):
    east, west, south, north, diagonal = operators
    return (
        diagonal * vector
        - east * padded[1:-1, 2:]
        - west * padded[1:-1, :-2]
        - south * padded[2:, 1:-1]
        - north * padded[:-2, 1:-1]
    )


def apply_halo(vector, operators):
    padded = extended(vector, (("az", 0), ("rg", 1)), 1)
    return combine_padded(vector, padded, operators)


def restrict_sum(vector):
    rows_now, cols_now = vector.shape
    return vector.reshape(rows_now // 2, 2, cols_now // 2, 2).sum(axis=(1, 3))


def prolong_copy(vector):
    rows_now, cols_now = vector.shape
    return jnp.broadcast_to(vector[:, None, :, None], (rows_now, 2, cols_now, 2)).reshape(
        rows_now * 2, cols_now * 2
    )


def build_levels(east, west, south, north, first_level):
    levels = [None] * first_level
    for level in range(first_level, LEVELS):
        diagonal = east + west + south + north + MU * 4.0**level
        levels.append((east, west, south, north, diagonal))
        if level + 1 < LEVELS:
            east, west, south, north = (
                east[0::2, 1::2] + east[1::2, 1::2],
                west[0::2, 0::2] + west[1::2, 0::2],
                south[1::2, 0::2] + south[1::2, 1::2],
                north[0::2, 0::2] + north[0::2, 1::2],
            )
    return levels


def jacobi_sweeps(rhs_vec, operators, apply_fn):
    estimate = OMEGA * rhs_vec / operators[4]
    for sweep_index in range(SWEEPS - 1):
        estimate = estimate + OMEGA * (rhs_vec - apply_fn(estimate, operators)) / operators[4]
    return estimate


def vcycle(rhs_vec, level, levels, coarse_fn, apply_fn, stop_level):
    if level == stop_level:
        return coarse_fn(rhs_vec)
    diagonal = levels[level][4]
    estimate = OMEGA * rhs_vec / diagonal
    remain = rhs_vec - apply_fn(estimate, levels[level])
    correction = vcycle(restrict_sum(remain), level + 1, levels, coarse_fn, apply_fn, stop_level)
    estimate = estimate + prolong_copy(correction)
    return estimate + OMEGA * (rhs_vec - apply_fn(estimate, levels[level])) / diagonal


def precond_norm(residual, precond):
    return lax.psum(jnp.sum(residual * precond), ("az", "rg"))


def local(master_phasor_raster, slave_phasor_raster, segment_track_trim, segment_slant_trim):
    n_az = lax.axis_size("az")
    n_range = lax.axis_size("rg")
    segment_ordinal = lax.axis_index("az")
    range_index = lax.axis_index("rg")
    track_trim_width = lax.dynamic_index_in_dim(
        segment_track_trim, segment_ordinal, 0, keepdims=False
    )
    slant_trim_width = lax.dynamic_index_in_dim(
        segment_slant_trim, segment_ordinal, 0, keepdims=False
    )
    slant_sample_total = COLS_DEV * n_range
    first_tile, second_tile = (
        lax.all_to_all(master_phasor_raster, "rg", split_axis=2, concat_axis=1, tiled=True),
        lax.all_to_all(slave_phasor_raster, "rg", split_axis=2, concat_axis=1, tiled=True),
    )
    along_track_position = jnp.arange(SEGMENT_HEIGHT, dtype=jnp.int32)
    column_index = range_index * COLS_DEV + jnp.arange(COLS_DEV, dtype=jnp.int32)
    pixel_totals = mean_multilook(
        first_tile,
        second_tile,
        along_track_position,
        column_index,
        track_trim_width,
        slant_trim_width,
        slant_sample_total,
    )
    look_re, look_im, power_one, power_two = (
        pixel_totals[0],
        pixel_totals[1],
        pixel_totals[2],
        pixel_totals[3],
    )
    weight = 0.05 + 4.0 * (look_re * look_re + look_im * look_im) / jnp.maximum(
        power_one * power_two, 1.0
    )
    shard_height_total, cols_here = weight.shape
    padded = extended(jnp.stack([look_re, look_im, weight]), (("az", 1), ("rg", 2)), 1)
    middle_h = padded[:, 1:-1, :]
    left_side = middle_h[:, :, :-1]
    right_side = middle_h[:, :, 1:]
    edge_h, grad_h = edge_terms(
        left_side[0], left_side[1], left_side[2], right_side[0], right_side[1], right_side[2]
    )
    left_global = range_index * cols_here - 1 + jnp.arange(cols_here + 1, dtype=jnp.int32)
    keep_h = ((left_global >= 0) & (left_global <= cols_here * n_range - 2)).astype(jnp.float32)
    edge_h = edge_h * keep_h[None, :]
    middle_v = padded[:, :, 1:-1]
    upper_side = middle_v[:, :-1, :]
    lower_side = middle_v[:, 1:, :]
    edge_v, grad_v = edge_terms(
        upper_side[0], upper_side[1], upper_side[2], lower_side[0], lower_side[1], lower_side[2]
    )
    upper_global_row = (
        segment_ordinal * shard_height_total
        - 1
        + jnp.arange(shard_height_total + 1, dtype=jnp.int32)
    )
    keep_v = ((upper_global_row >= 0) & (upper_global_row <= shard_height_total * n_az - 2)).astype(
        jnp.float32
    )
    edge_v = edge_v * keep_v[:, None]
    flux_h = edge_h * grad_h
    flux_v = edge_v * grad_v
    rhs = -(flux_h[:, 1:] - flux_h[:, :-1] + flux_v[1:, :] - flux_v[:-1, :])
    levels = build_levels(edge_h[:, 1:], edge_h[:, :-1], edge_v[1:, :], edge_v[:-1, :], 0)
    stop_level = LEVELS - 1

    def coarse_fn(rhs_vec):
        return jacobi_sweeps(rhs_vec, levels[LEVELS - 1], apply_halo)

    def precondition(vector):
        return vcycle(vector, 0, levels, coarse_fn, apply_halo, stop_level)

    solution = jnp.zeros_like(rhs)
    residual = rhs
    precond = precondition(residual)
    direction = precond
    norm_now = precond_norm(residual, precond)
    for step_index in range(ITERS):
        image_vec = apply_halo(direction, levels[0])
        step_length = norm_now / lax.psum(jnp.sum(direction * image_vec), ("az", "rg"))
        solution = solution + step_length * direction
        residual = residual - step_length * image_vec
        if step_index + 1 < ITERS:
            precond = precondition(residual)
            norm_next = precond_norm(residual, precond)
            direction = precond + norm_next / norm_now * direction
            norm_now = norm_next
    return (solution, weight)


def solution(mesh):
    return jax.shard_map(
        local,
        mesh=mesh,
        in_specs=(P(None, ("az", "rg"), None), P(None, ("az", "rg"), None), P(), P()),
        out_specs=(P("az", "rg"), P("az", "rg")),
        check_vma=False,
    )
```

profile of v0, /device:TPU:1, one launch (start us, length us, event | category | flops | bytes accessed | tf_op | source)
XLA Modules:
  0.0 1362.9 jit_solution(13739139236446719349)
XLA Ops:
  0.6 10.7 copy.56
  11.4 10.8 reshape.488
  27.9 8.2 copy.59
  36.1 10.7 reshape.486
  56.1 14.1 %reshape.489 = bf16[10240,2,20]{2,1,0:T(2,128)(2,1)} reshape(bf16[8,2,25600]{2,1,0:T(2,128)(2,1)S(1)} %all-to-all-done) | data formatting | bytes 1638400
  70.2 10.3 copy.57
  84.8 22.2 %reshape.470 = f32[1,32,5,256,5]{4,3,0,2,1:T(8,128)} reshape(f32[8,20,1280]{2,1,0:T(8,128)S(1)} %get-tuple-element.3) | data formatting | bytes 1638400 | tf_op jit(solution)/shard_map/convert_element_type | solution.py:51
  107.0 12.2 copy.58
  119.2 15.1 %reshape.487 = bf16[10240,2,20]{2,1,0:T(2,128)(2,1)} reshape(bf16[8,2,25600]{2,1,0:T(2,128)(2,1)} %all-to-all-done.1) | data formatting | bytes 1638400
  134.3 10.5 copy.60
  150.1 23.1 %reshape.471 = f32[1,32,5,256,5]{4,3,0,2,1:T(8,128)} reshape(f32[8,20,1280]{2,1,0:T(8,128)} %get-tuple-element.5) | data formatting | bytes 1638400 | tf_op jit(solution)/shard_map/convert_element_type | solution.py:53
  173.2 12.2 copy.61
  185.4 22.2 %reshape.472 = f32[1,32,5,256,5]{4,3,0,2,1:T(8,128)} reshape(f32[8,20,1280]{2,1,0:T(8,128)S(1)} %get-tuple-element.2) | data formatting | bytes 1638400 | tf_op jit(solution)/shard_map/convert_element_type | solution.py:52
  207.6 12.2 copy.62
  219.9 22.2 %reshape.473 = f32[1,32,5,256,5]{4,3,0,2,1:T(8,128)} reshape(f32[8,20,1280]{2,1,0:T(8,128)S(1)} %get-tuple-element.4) | data formatting | bytes 1638400 | tf_op jit(solution)/shard_map/convert_element_type | solution.py:54
  242.1 11.6 copy.63
  468.4 6.0 collective-permute-start.48
  527.3 67.4 %all-reduce = (f32[]{:T(128)}, f32[]{:T(128)}) all-reduce(f32[]{:T(128)} %get-tuple-element.7, f32[]{:T(128)} %get-tuple-element.6), channel_id=1, replica_groups=mesh['az'=16,'rg'=8] {'az','rg'}, use_global_device_ids=true, to_apply=%region_8.9 | all-reduce | flops 2 | bytes 16 | tf_op jit(solution)/shard_map/psum | solution.py:138
  784.9 6.0 collective-permute-start.104
  827.0 66.1 %psum.44 = f32[]{:T(128)} all-reduce(f32[]{:T(128)} %get-tuple-element.16), channel_id=1, replica_groups=mesh['az'=16,'rg'=8] {'az','rg'}, use_global_device_ids=true, to_apply=%region_18.19 | all-reduce | flops 1 | bytes 8 | tf_op jit(solution)/shard_map/psum | solution.py:138
  911.5 66.2 %psum.45 = f32[]{:T(128)} all-reduce(f32[]{:T(128)} %get-tuple-element.14), channel_id=1, replica_groups=mesh['az'=16,'rg'=8] {'az','rg'}, use_global_device_ids=true, to_apply=%region_20.21 | all-reduce | flops 1 | bytes 8 | tf_op jit(solution)/shard_map/psum | solution.py:222
  1167.7 6.0 collective-permute-start.160
  1209.8 66.1 %psum.46 = f32[]{:T(128)} all-reduce(f32[]{:T(128)} %get-tuple-element.10), channel_id=1, replica_groups=mesh['az'=16,'rg'=8] {'az','rg'}, use_global_device_ids=true, to_apply=%region_28.29 | all-reduce | flops 1 | bytes 8 | tf_op jit(solution)/shard_map/psum | solution.py:138
  1294.7 66.1 %psum.47 = f32[]{:T(128)} all-reduce(f32[]{:T(128)} %fusion.17), channel_id=1, replica_groups=mesh['az'=16,'rg'=8] {'az','rg'}, use_global_device_ids=true, to_apply=%region_30.31 | all-reduce | flops 1 | bytes 8 | tf_op jit(solution)/shard_map/psum | solution.py:222
  (713 shorter events, 772.7 us)
Async XLA Ops:
  22.1 25.3 %all-to-all-start = ((bf16[8,2,25600]{2,1,0:T(2,128)(2,1)}), bf16[8,2,25600]{2,1,0:T(2,128)(2,1)S(1)}, u32[]{:S(2)}, u32[]{:S(2)}) async-start(bf16[8,2,25600]{2,1,0:T(2,128)(2,1)} %reshape.488), calls=%async_computation | async-start | bytes 1638400 | tf_op jit(solution)/shard_map/all_to_all | solution.py:154
  47.5 71.8 %all-to-all-start.1 = ((bf16[8,2,25600]{2,1,0:T(2,128)(2,1)}), bf16[8,2,25600]{2,1,0:T(2,128)(2,1)}, u32[]{:S(2)}, u32[]{:S(2)}) async-start(bf16[8,2,25600]{2,1,0:T(2,128)(2,1)} %reshape.486), calls=%async_computation.1 | async-start | bytes 1638400 | tf_op jit(solution)/shard_map/all_to_all | solution.py:155
  269.2 7.6 collective-permute-start.4
  277.5 8.0 collective-permute-start.7
  311.4 7.5 collective-permute-start.12
  370.4 7.3 collective-permute-start.26
  391.3 7.3 collective-permute-start.30
  409.8 7.3 collective-permute-start.34
  457.6 7.3 collective-permute-start.47
  468.4 7.3 collective-permute-start.48
  491.2 7.1 collective-permute-start.52
  686.9 7.3 collective-permute-start.82
  707.7 7.3 collective-permute-start.86
  726.3 7.3 collective-permute-start.90
  774.1 7.3 collective-permute-start.103
  784.9 7.3 collective-permute-start.104
  807.6 7.1 collective-permute-start.108
  900.5 7.1 collective-permute-start.115
  1069.6 7.3 collective-permute-start.138
  1090.5 7.3 collective-permute-start.142
  1109.0 7.3 collective-permute-start.146
  1156.8 7.3 collective-permute-start.159
  1167.7 7.3 collective-permute-start.160
  1283.0 7.1 collective-permute-start.171
  (156 other events, 896.7 us)
where the time goes:
time: 1370 us; the launch traced here: 1360 us
  starting transfers between devices  530 us (39%)
  blocking collectives  332 us (24%)
  local copies, waits for them, and re-layouts  256 us (19%)
  waiting for transfers between devices  208 us (15%)
  other arithmetic  25 us (2%)
    ppermute x86, starting transfers between devices, extended(): lax.ppermute(tail, axis, [(i, (i + 1) % count) for i in range(ends)])  379 us
    psum x3, blocking collectives, precond_norm(): return lax.psum(jnp.sum(residual * precond), ('az', 'rg'))  200 us
    ppermute x86, waiting for transfers between devices, extended(): lax.ppermute(head, axis, [((i + 1) % count, i) for i in range(ends)])  184 us
    ppermute x86, starting transfers between devices, extended(): lax.ppermute(head, axis, [((i + 1) % count, i) for i in range(ends)])  139 us
    psum x2, blocking collectives, local(): lax.psum(jnp.sum(direction * image_vec), ('az', 'rg'))  132 us
    unnamed x20, local copies, waits for them, and re-layouts  70.3 us
    convert_element_type x2, local copies, waits for them, and re-layouts, mean_multilook(): second_re = trailing_phasor_raster[0].astype(jnp.float32) * valid_mask  35.3 us
    convert_element_type x2, local copies, waits for them, and re-layouts, mean_multilook(): first_re = leading_phasor_raster[0].astype(jnp.float32) * valid_mask  34.5 us
  transfers between devices with their start and end apart: 174, of which 86 were waited for; matrix products, arithmetic and copies ran while one was open for 7% of the time, Pallas kernels for 0%

commit v1 on v0

v1 whole, which is shorter than its diff:
```python
import jax
import jax.numpy as jnp
from jax import lax
from jax.sharding import PartitionSpec as P

LOOK = 5
LEVELS = 6
ITERS = 3
SWEEPS = 4
SEGMENT_HEIGHT = 160
GATHER_LEVEL = 2


OMEGA = 0.6
MU = 0.01


def neighbours(v):
    n_az = lax.axis_size("az")
    n_rg = lax.axis_size("rg")
    above = lax.ppermute(v[..., -1:, :], "az", [(i, i + 1) for i in range(n_az - 1)])
    below = lax.ppermute(v[..., :1, :], "az", [(i + 1, i) for i in range(n_az - 1)])
    left = lax.ppermute(v[..., :, -1:], "rg", [(i, i + 1) for i in range(n_rg - 1)])
    right = lax.ppermute(v[..., :, :1], "rg", [(i + 1, i) for i in range(n_rg - 1)])
    north = jnp.concatenate([above, v[..., :-1, :]], axis=-2)
    south = jnp.concatenate([v[..., 1:, :], below], axis=-2)
    west = jnp.concatenate([left, v[..., :, :-1]], axis=-1)
    east = jnp.concatenate([v[..., :, 1:], right], axis=-1)
    return north, south, west, east


def apply_halo(vector, operators):
    east, west, south, north, diagonal = operators
    v_n, v_s, v_w, v_e = neighbours(vector)
    return diagonal * vector - east * v_e - west * v_w - south * v_s - north * v_n


def apply_padded(vector, operators):
    east, west, south, north, diagonal = operators
    padded = jnp.pad(vector, 1)
    return (diagonal * vector - east * padded[1:-1, 2:] - west * padded[1:-1, :-2]
            - south * padded[2:, 1:-1] - north * padded[:-2, 1:-1])


def mean_multilook(leading, trailing, row_ok, col_ok):
    valid_mask = (row_ok[:, None] & col_ok[None, :]).astype(jnp.float32)
    first_re = leading[0].astype(jnp.float32) * valid_mask
    first_im = leading[1].astype(jnp.float32) * valid_mask
    second_re = trailing[0].astype(jnp.float32) * valid_mask
    second_im = trailing[1].astype(jnp.float32) * valid_mask
    products = jnp.stack(
        [
            first_re * second_re + first_im * second_im,
            first_im * second_re - first_re * second_im,
            first_re * first_re + first_im * first_im,
            second_re * second_re + second_im * second_im,
        ]
    )
    height_rows, width_cols = valid_mask.shape
    rows = products.reshape(4, height_rows // LOOK, LOOK, width_cols).sum(axis=2)
    return rows.reshape(4, height_rows // LOOK, width_cols // LOOK, LOOK).sum(axis=3)


def edge_terms(left_re, left_im, left_weight, right_re, right_im, right_weight):
    edge_weight = 0.5 * (left_weight + right_weight)
    cross_im = right_im * left_re - right_re * left_im
    power_sum = (
        left_re * left_re + left_im * left_im + right_re * right_re + right_im * right_im + 1.0
    )
    return (edge_weight, 2.0 * cross_im / power_sum)


def restrict_sum(vector):
    rows_now, cols_now = vector.shape
    return vector.reshape(rows_now // 2, 2, cols_now // 2, 2).sum(axis=(1, 3))


def prolong_copy(vector):
    rows_now, cols_now = vector.shape
    return jnp.broadcast_to(vector[:, None, :, None], (rows_now, 2, cols_now, 2)).reshape(
        rows_now * 2, cols_now * 2
    )


def coarsen(east, west, south, north):
    return (
        east[0::2, 1::2] + east[1::2, 1::2],
        west[0::2, 0::2] + west[1::2, 0::2],
        south[1::2, 0::2] + south[1::2, 1::2],
        north[0::2, 0::2] + north[0::2, 1::2],
    )


def build_levels(east, west, south, north, first_level, last_level):
    levels = {}
    for level in range(first_level, last_level):
        diagonal = east + west + south + north + MU * 4.0**level
        levels[level] = (east, west, south, north, diagonal)
        if level + 1 < LEVELS:
            east, west, south, north = coarsen(east, west, south, north)
    return levels, (east, west, south, north)


def jacobi_sweeps(rhs_vec, operators, apply_fn):
    estimate = OMEGA * rhs_vec / operators[4]
    for sweep_index in range(SWEEPS - 1):
        estimate = estimate + OMEGA * (rhs_vec - apply_fn(estimate, operators)) / operators[4]
    return estimate


def vcycle(rhs_vec, level, levels, apply_fn, stop_fn):
    if level == LEVELS - 1:
        return jacobi_sweeps(rhs_vec, levels[level], apply_fn)
    if stop_fn is not None and level == GATHER_LEVEL:
        return stop_fn(rhs_vec)
    diagonal = levels[level][4]
    estimate = OMEGA * rhs_vec / diagonal
    remain = rhs_vec - apply_fn(estimate, levels[level])
    correction = vcycle(restrict_sum(remain), level + 1, levels, apply_fn, stop_fn)
    estimate = estimate + prolong_copy(correction)
    return estimate + OMEGA * (rhs_vec - apply_fn(estimate, levels[level])) / diagonal


def everyone():
    return lax.axis_size("az") * lax.axis_size("rg")


def gather_grid(blocks):
    n_az = lax.axis_size("az")
    n_rg = lax.axis_size("rg")
    count, h, w = blocks.shape
    sent = jnp.broadcast_to(blocks[None], (n_az * n_rg, count, h, w))
    got = lax.all_to_all(sent, ("az", "rg"), 0, 0, tiled=True)
    got = got.reshape(n_az, n_rg, count, h, w).transpose(2, 0, 3, 1, 4)
    return got.reshape(count, n_az * h, n_rg * w)


def total(values):
    n = everyone()
    sent = jnp.broadcast_to(values[None], (n, values.shape[0]))
    got = lax.all_to_all(sent, ("az", "rg"), 0, 0, tiled=True)
    return jnp.sum(got, axis=0)


def local(master_phasor_raster, slave_phasor_raster, segment_track_trim, segment_slant_trim):
    n_az = lax.axis_size("az")
    n_range = lax.axis_size("rg")
    segment_ordinal = lax.axis_index("az")
    range_index = lax.axis_index("rg")
    track_trim_width = lax.dynamic_index_in_dim(
        segment_track_trim, segment_ordinal, 0, keepdims=False
    )
    slant_trim_width = lax.dynamic_index_in_dim(
        segment_slant_trim, segment_ordinal, 0, keepdims=False
    )
    lines_here = master_phasor_raster.shape[1]
    slant_sample_total = master_phasor_raster.shape[2]
    along_track_position = range_index * lines_here + jnp.arange(lines_here, dtype=jnp.int32)
    column_index = jnp.arange(slant_sample_total, dtype=jnp.int32)
    row_ok = (along_track_position >= track_trim_width[0]) & (
        along_track_position < SEGMENT_HEIGHT - track_trim_width[1]
    )
    col_ok = (column_index >= slant_trim_width[0]) & (
        column_index < slant_sample_total - slant_trim_width[1]
    )
    pixel_totals = mean_multilook(master_phasor_raster, slave_phasor_raster, row_ok, col_ok)
    look_re, look_im, power_one, power_two = (
        pixel_totals[0],
        pixel_totals[1],
        pixel_totals[2],
        pixel_totals[3],
    )
    weight = 0.05 + 4.0 * (look_re * look_re + look_im * look_im) / jnp.maximum(
        power_one * power_two, 1.0
    )
    fields = jnp.stack([look_re, look_im, weight])
    n_fields, rows_here, cols_all = fields.shape
    cols_here = cols_all // n_range
    fields = fields.reshape(n_fields, rows_here, n_range, cols_here).transpose(2, 0, 1, 3)
    fields = lax.all_to_all(fields, "rg", 0, 0, tiled=True)
    fields = fields.transpose(1, 0, 2, 3).reshape(n_fields, n_range * rows_here, cols_here)
    weight = fields[2]
    shard_height_total = n_range * rows_here

    f_n, f_s, f_w, f_e = neighbours(fields)
    edge_h, grad_h = edge_terms(fields[0], fields[1], fields[2], f_e[0], f_e[1], f_e[2])
    col_global = range_index * cols_here + jnp.arange(cols_here, dtype=jnp.int32)
    keep_h = (col_global <= cols_here * n_range - 2).astype(jnp.float32)
    edge_h = edge_h * keep_h[None, :]
    edge_v, grad_v = edge_terms(fields[0], fields[1], fields[2], f_s[0], f_s[1], f_s[2])
    row_global = segment_ordinal * shard_height_total + jnp.arange(shard_height_total, dtype=jnp.int32)
    keep_v = (row_global <= shard_height_total * n_az - 2).astype(jnp.float32)
    edge_v = edge_v * keep_v[:, None]
    flux_h = edge_h * grad_h
    flux_v = edge_v * grad_v
    e_n, _, e_w, _ = neighbours(jnp.stack([edge_h, flux_h, edge_v, flux_v]))
    west_edge, flux_w, north_edge, flux_n = e_w[0], e_w[1], e_n[2], e_n[3]
    rhs = -(flux_h - flux_w + flux_v - flux_n)

    levels, coarse_edges = build_levels(edge_h, west_edge, south=edge_v, north=north_edge,
                                        first_level=0, last_level=GATHER_LEVEL)
    whole_edges = gather_grid(jnp.stack(coarse_edges))
    whole_levels, _ = build_levels(whole_edges[0], whole_edges[1], whole_edges[2], whole_edges[3],
                                   GATHER_LEVEL, LEVELS)
    block_h, block_w = coarse_edges[0].shape

    def coarse_solve(rhs_vec):
        whole_rhs = gather_grid(rhs_vec[None])[0]
        whole_x = vcycle(whole_rhs, GATHER_LEVEL, whole_levels, apply_padded, None)
        return lax.dynamic_slice(whole_x, (segment_ordinal * block_h, range_index * block_w),
                                 (block_h, block_w))

    def precondition(vector):
        return vcycle(vector, 0, levels, apply_halo, coarse_solve)

    solution = jnp.zeros_like(rhs)
    residual = rhs
    precond = precondition(residual)
    direction = precond
    image_vec = apply_halo(direction, levels[0])
    sums = total(jnp.stack([jnp.sum(residual * precond), jnp.sum(direction * image_vec)]))
    norm_now = sums[0]
    curvature = sums[1]
    for step_index in range(ITERS):
        if step_index > 0:
            image_vec = apply_halo(direction, levels[0])
            curvature = total(jnp.sum(direction * image_vec)[None])[0]
        step_length = norm_now / curvature
        solution = solution + step_length * direction
        residual = residual - step_length * image_vec
        if step_index + 1 < ITERS:
            precond = precondition(residual)
            norm_next = total(jnp.sum(residual * precond)[None])[0]
            direction = precond + norm_next / norm_now * direction
            norm_now = norm_next
    return (solution, weight)


def solution(mesh):
    return jax.shard_map(
        local,
        mesh=mesh,
        in_specs=(P(None, ("az", "rg"), None), P(None, ("az", "rg"), None), P(), P()),
        out_specs=(P("az", "rg"), P("az", "rg")),
        check_vma=False,
    )
```

time: 1370 us -> 912 us (0.67)
  starting transfers between devices: 530 us -> 231 us
  blocking collectives: 332 us -> 63.5 us
  local copies, waits for them, and re-layouts: 256 us -> 425 us
  waiting for transfers between devices: 208 us -> 65 us
  other arithmetic: 25 us -> 107 us
    ppermute x172 -> x64, starting transfers between devices: 519 us -> 164 us  [the longest x16 57.5 us: neighbours(): lax.ppermute(v[..., -1:, :], 'az', [(i, i + 1) for i in range(n_az - 1)])]
    psum x5 -> x0, blocking collectives: 332 us -> none  [the longest x3 200 us: precond_norm(): return lax.psum(jnp.sum(residual * precond), ('az', 'rg'))]
    ppermute x172 -> x64, waiting for transfers between devices: 208 us -> 27.8 us  [the longest x16 25.9 us: neighbours(): lax.ppermute(v[..., :, :1], 'rg', [(i + 1, i) for i in range(n_rg - 1)])]
    convert_element_type x8 -> x0, local copies, waits for them, and re-layouts: 138 us -> none  [the longest x2 35.3 us: mean_multilook(): second_re = trailing_phasor_raster[0].astype(jnp.float32) * valid_mask]
    concatenate x0 -> x56, local copies, waits for them, and re-layouts: none -> 116 us  [the longest x14 30.2 us: neighbours(): west = jnp.concatenate([left, v[..., :, :-1]], axis=-1)]
    reshape x12, local copies, waits for them, and re-layouts: 8.33 us -> 76.8 us  [restrict_sum(): return vector.reshape(rows_now // 2, 2, cols_now // 2, 2).sum(axis=(1, 3))]
    unnamed x20 -> x203, local copies, waits for them, and re-layouts: 70.3 us -> 6.78 us
    all_to_all x0 -> x3, blocking collectives: none -> 63.5 us  [the longest x2 46.6 us: gather_grid(): got = lax.all_to_all(sent, ('az', 'rg'), 0, 0, tiled=True)]
  transfers between devices with their start and end apart: 174 -> 71, of which waited for: 86 -> 18; matrix products, arithmetic and copies ran while one was open for 7% -> 18% of each run, Pallas kernels for 0% -> 0%
where the time goes in v1:
time: 912 us; the launch traced here: 904 us
  local copies, waits for them, and re-layouts  425 us (47%)
  starting transfers between devices  231 us (25%)
  other arithmetic  107 us (12%)
  waiting for transfers between devices  65 us (7%)
  blocking collectives  63.5 us (7%)
  between operations  11.9 us (1%)
    reshape x12, local copies, waits for them, and re-layouts, restrict_sum(): return vector.reshape(rows_now // 2, 2, cols_now // 2, 2).sum(axis=(1, 3))  76.8 us
    reshape x15, local copies, waits for them, and re-layouts, prolong_copy(): jnp.broadcast_to(vector[:, None, :, None], (rows_now, 2, cols_now, 2))  59.3 us
    ppermute x16, starting transfers between devices, neighbours(): lax.ppermute(v[..., -1:, :], 'az', [(i, i + 1) for i in range(n_az - 1)])  57.5 us
    ppermute x16, starting transfers between devices, neighbours(): lax.ppermute(v[..., :, -1:], 'rg', [(i, i + 1) for i in range(n_rg - 1)])  47.2 us
    all_to_all x2, blocking collectives, gather_grid(): got = lax.all_to_all(sent, ('az', 'rg'), 0, 0, tiled=True)  46.6 us
    all_to_all x4, starting transfers between devices, total(): got = lax.all_to_all(sent, ('az', 'rg'), 0, 0, tiled=True)  43.3 us
    ppermute x16, starting transfers between devices, neighbours(): lax.ppermute(v[..., :, :1], 'rg', [(i + 1, i) for i in range(n_rg - 1)])  38.4 us
    reduce_sum x15, other arithmetic, restrict_sum(): return vector.reshape(rows_now // 2, 2, cols_now // 2, 2).sum(axis=(1, 3))  37.9 us
  transfers between devices with their start and end apart: 71, of which 18 were waited for; matrix products, arithmetic and copies ran while one was open for 18% of the time, Pallas kernels for 0%

profile of v1, /device:TPU:1, one launch (start us, length us, event | category | flops | bytes accessed | tf_op | source)
XLA Modules:
  0.0 903.7 jit_solution(7660379944790419260)
XLA Ops:
  17.2 19.2 %reshape.882 = f32[4,4,2048,5]{3,2,1,0:T(8,128)} reshape(f32[4,4,10240]{2,1,0:T(4,128)S(1)} %copy.59) | data formatting | bytes 1310720 | tf_op jit(solution)/shard_map/reshape | solution.py:61
  36.3 8.2 reduce_sum.253
  104.9 12.9 %squeeze.146 = f32[16,2,128,2]{3,2,1,0:T(8,128)S(1)} reshape(f32[1,32,256]{2,1,0:T(8,128)S(1)} %get-tuple-element.61) | data formatting | bytes 65536 | tf_op jit(solution)/shard_map/squeeze | solution.py:197
  169.7 13.6 %all-to-all-start.1 = ((f32[128,1,512]{2,1,0:T(1,128)}), f32[128,1,512]{2,1,0:T(1,128)S(1)}, u32[]{:S(2)}, u32[]{:S(2)}) async-start(f32[128,1,512]{2,1,0:T(1,128)} %reshape.923), calls=%async_computation.1 | async-start | bytes 524288 | tf_op jit(solution)/shard_map/all_to_all | solution.py:133
  185.9 8.5 all-to-all-done.1
  202.7 15.5 %all-to-all-done.2 = f32[128,1,2048]{2,1,0:T(1,128)S(1)} async-done(((f32[128,1,2048]{2,1,0:T(1,128)}), f32[128,1,2048]{2,1,0:T(1,128)S(1)}, u32[]{:S(2)}, u32[]{:S(2)}) %all-to-all-start.2) | async-done | bytes 1048608 | tf_op jit(solution)/shard_map/all_to_all | solution.py:133
  242.8 18.3 %reshape.887 = f32[64,2,256,2]{3,2,1,0:T(8,128)} reshape(f32[128,512]{1,0:T(8,128)S(1)} %fusion.5) | data formatting | bytes 524288 | tf_op jit(solution)/shard_map/reshape | solution.py:75
  261.2 8.0 reduce_sum.256
  298.5 6.6 broadcast_in_dim.58
  305.2 12.7 %reshape.892 = f32[128,512]{1,0:T(8,128)S(1)} reshape(f32[64,2,256,2]{3,2,1,0:T(8,128)} %broadcast_in_dim.58) | data formatting | bytes 524288 | tf_op jit(solution)/shard_map/reshape | solution.py:80
  368.5 12.9 %all-to-all-start.3 = ((f32[128,1,2]{2,1,0:T(1,128)}), f32[128,1,2]{2,1,0:T(1,128)}, u32[]{:S(2)}, u32[]{:S(2)}) async-start(f32[128,1,2]{2,1,0:T(1,128)} %broadcast_in_dim.62), calls=%async_computation.3 | async-start | bytes 131072 | tf_op jit(solution)/shard_map/all_to_all | solution.py:141
  477.1 23.4 %all_to_all.55 = f32[128,1,512]{2,1,0:T(1,128)S(1)} all-to-all(f32[128,1,512]{2,1,0:T(1,128)S(1)} %reshape.925), channel_id=1, replica_groups=mesh['az'=16,'rg'=8] {'az','rg'}, dimensions={0} | all-to-all | bytes 524288 | tf_op jit(solution)/shard_map/all_to_all | solution.py:133
  502.4 18.1 %reshape.897 = f32[64,2,256,2]{3,2,1,0:T(8,128)} reshape(f32[128,512]{1,0:T(8,128)S(1)} %fusion.19) | data formatting | bytes 524288 | tf_op jit(solution)/shard_map/reshape | solution.py:75
  520.6 8.0 reduce_sum.264
  553.1 12.9 %reshape.902 = f32[128,512]{1,0:T(8,128)S(1)} reshape(f32[64,2,256,2]{3,2,1,0:T(8,128)} %broadcast_in_dim.66) | data formatting | bytes 524288 | tf_op jit(solution)/shard_map/reshape | solution.py:80
  601.8 9.9 %all-to-all-start.5 = ((f32[128,1,1]{2,1,0:T(1,128)}), f32[128,1,1]{2,1,0:T(1,128)}, u32[]{:S(2)}, u32[]{:S(2)}) async-start(f32[128,1,1]{2,1,0:T(1,128)} %broadcast_in_dim.69), calls=%async_computation.5 | async-start | bytes 131072 | tf_op jit(solution)/shard_map/all_to_all | solution.py:141
  648.6 10.7 %all-to-all-start.6 = ((f32[128,1,1]{2,1,0:T(1,128)}), f32[128,1,1]{2,1,0:T(1,128)}, u32[]{:S(2)}, u32[]{:S(2)}) async-start(f32[128,1,1]{2,1,0:T(1,128)} %broadcast_in_dim.71), calls=%async_computation.6 | async-start | bytes 131072 | tf_op jit(solution)/shard_map/all_to_all | solution.py:141
  731.3 23.2 %all_to_all.56 = f32[128,1,512]{2,1,0:T(1,128)S(1)} all-to-all(f32[128,1,512]{2,1,0:T(1,128)S(1)} %reshape.927), channel_id=1, replica_groups=mesh['az'=16,'rg'=8] {'az','rg'}, dimensions={0} | all-to-all | bytes 524288 | tf_op jit(solution)/shard_map/all_to_all | solution.py:133
  756.4 18.1 %reshape.907 = f32[64,2,256,2]{3,2,1,0:T(8,128)} reshape(f32[128,512]{1,0:T(8,128)S(1)} %fusion.33) | data formatting | bytes 524288 | tf_op jit(solution)/shard_map/reshape | solution.py:75
  774.5 8.0 reduce_sum.273
  807.1 12.9 %reshape.912 = f32[128,512]{1,0:T(8,128)S(1)} reshape(f32[64,2,256,2]{3,2,1,0:T(8,128)} %broadcast_in_dim.75) | data formatting | bytes 524288 | tf_op jit(solution)/shard_map/reshape | solution.py:80
  849.0 9.8 %all-to-all-start.8 = ((f32[128,1,1]{2,1,0:T(1,128)}), f32[128,1,1]{2,1,0:T(1,128)S(1)}, u32[]{:S(2)}, u32[]{:S(2)}) async-start(f32[128,1,1]{2,1,0:T(1,128)} %broadcast_in_dim.78), calls=%async_computation.8 | async-start | bytes 131072 | tf_op jit(solution)/shard_map/all_to_all | solution.py:141
  860.0 8.4 all-to-all-done.8
  883.9 16.9 %all_to_all.57 = f32[128,1,1]{2,1,0:T(1,128)S(1)} all-to-all(f32[128,1,1]{2,1,0:T(1,128)S(1)} %broadcast_in_dim.80), channel_id=1, replica_groups=mesh['az'=16,'rg'=8] {'az','rg'}, dimensions={0} | all-to-all | bytes 1024 | tf_op jit(solution)/shard_map/all_to_all | solution.py:141
  (738 shorter events, 574.9 us)
Async XLA Ops:
  56.2 17.2 %collective-permute-start.1 = (f32[3,1,256]{2,1,0:T(1,128)S(1)}, f32[3,1,256]{2,1,0:T(1,128)S(1)}, u32[]{:S(2)}, u32[]{:S(2)}) collective-permute-start(f32[3,1,256]{2,1,0:T(1,128)S(1)} %slice.1262), channel_id=1, source_target_pairs={{8,0},{16,8},{24,16},{32,24},{40,32},{48,40},{56,48},{64,56},{72,6... | collective-permute-start | bytes 9224 | tf_op jit(solution)/shard_map/ppermute | solution.py:22
  57.7 15.7 %collective-permute-start = (f32[3,32,1]{2,1,0:T(8,128)S(1)}, f32[3,32,1]{2,1,0:T(8,128)S(1)}, u32[]{:S(2)}, u32[]{:S(2)}) collective-permute-start(f32[3,32,1]{2,1,0:T(8,128)S(1)} %slice.1254), channel_id=1, source_target_pairs={{1,0},{2,1},{3,2},{4,3},{5,4},{6,5},{7,6},{9,8},{10,9},{11,10},{12... | collective-permute-start | bytes 1160 | tf_op jit(solution)/shard_map/ppermute | solution.py:24
  74.2 23.5 %collective-permute-start.3 = (f32[4,1,256]{2,1,0:T(1,128)S(1)}, f32[4,1,256]{2,1,0:T(1,128)S(1)}, u32[]{:S(2)}, u32[]{:S(2)}) collective-permute-start(f32[4,1,256]{2,1,0:T(1,128)S(1)} %pad_maximum_fusion.40), channel_id=1, source_target_pairs={{0,8},{8,16},{16,24},{24,32},{32,40},{40,48},{48,56},{56,64},{64,7... | collective-permute-start | bytes 12296 | tf_op jit(solution)/shard_map/ppermute | solution.py:21
  78.5 19.2 %collective-permute-start.2 = (f32[4,32,1]{2,1,0:T(8,128)S(1)}, f32[4,32,1]{2,1,0:T(8,128)S(1)}, u32[]{:S(2)}, u32[]{:S(2)}) collective-permute-start(f32[4,32,1]{2,1,0:T(8,128)S(1)} %slice.1267), channel_id=1, source_target_pairs={{0,1},{1,2},{2,3},{3,4},{4,5},{5,6},{6,7},{8,9},{9,10},{10,11},{11... | collective-permute-start | bytes 1544 | tf_op jit(solution)/shard_map/ppermute | solution.py:23
  117.8 33.5 %collective-permute-start.6 = (f32[1,256]{1,0:T(1,128)S(1)}, f32[1,256]{1,0:T(1,128)S(1)}, u32[]{:S(2)}, u32[]{:S(2)}) collective-permute-start(f32[1,256]{1,0:T(1,128)S(1)} %get-tuple-element.182), channel_id=1, source_target_pairs={{8,0},{16,8},{24,16},{32,24},{40,32},{48,40},{56,48},{64,56},{72,6... | collective-permute-start | bytes 3080 | tf_op jit(solution)/shard_map/ppermute | solution.py:22
  119.1 29.4 %collective-permute-start.7 = (f32[1,256]{1,0:T(1,128)S(1)}, f32[1,256]{1,0:T(1,128)S(1)}, u32[]{:S(2)}, u32[]{:S(2)}) collective-permute-start(f32[1,256]{1,0:T(1,128)S(1)} %get-tuple-element.183), channel_id=1, source_target_pairs={{0,8},{8,16},{16,24},{24,32},{32,40},{40,48},{48,56},{56,64},{64,7... | collective-permute-start | bytes 3080 | tf_op jit(solution)/shard_map/ppermute | solution.py:21
  123.1 19.8 %collective-permute-start.4 = (f32[32,1]{1,0:T(8,128)S(1)}, f32[32,1]{1,0:T(8,128)S(1)}, u32[]{:S(2)}, u32[]{:S(2)}) collective-permute-start(f32[32,1]{1,0:T(8,128)S(1)} %get-tuple-element.178), channel_id=1, source_target_pairs={{1,0},{2,1},{3,2},{4,3},{5,4},{6,5},{7,6},{9,8},{10,9},{11,10},{12... | collective-permute-start | bytes 392 | tf_op jit(solution)/shard_map/ppermute | solution.py:24
  125.2 17.8 %collective-permute-start.5 = (f32[32,1]{1,0:T(8,128)S(1)}, f32[32,1]{1,0:T(8,128)S(1)}, u32[]{:S(2)}, u32[]{:S(2)}) collective-permute-start(f32[32,1]{1,0:T(8,128)S(1)} %get-tuple-element.179), channel_id=1, source_target_pairs={{0,1},{1,2},{2,3},{3,4},{4,5},{5,6},{6,7},{8,9},{9,10},{10,11},{11... | collective-permute-start | bytes 392 | tf_op jit(solution)/shard_map/ppermute | solution.py:23
  169.7 24.7 %all-to-all-start.1 = ((f32[128,1,512]{2,1,0:T(1,128)}), f32[128,1,512]{2,1,0:T(1,128)S(1)}, u32[]{:S(2)}, u32[]{:S(2)}) async-start(f32[128,1,512]{2,1,0:T(1,128)} %reshape.923), calls=%async_computation.1 | async-start | bytes 524288 | tf_op jit(solution)/shard_map/all_to_all | solution.py:133
  194.4 23.8 %all-to-all-start.2 = ((f32[128,1,2048]{2,1,0:T(1,128)}), f32[128,1,2048]{2,1,0:T(1,128)S(1)}, u32[]{:S(2)}, u32[]{:S(2)}) async-start(f32[128,1,2048]{2,1,0:T(1,128)} %reshape.921), calls=%async_computation.2 | async-start | bytes 2097152 | tf_op jit(solution)/shard_map/all_to_all | solution.py:133
  335.0 14.4 %collective-permute-start.19 = (f32[1,256]{1,0:T(1,128)}, f32[1,256]{1,0:T(1,128)}, u32[]{:S(2)}, u32[]{:S(2)}) collective-permute-start(f32[1,256]{1,0:T(1,128)} %get-tuple-element.168), channel_id=1, source_target_pairs={{0,8},{8,16},{16,24},{24,32},{32,40},{40,48},{48,56},{56,64},{64,7... | collective-permute-start | bytes 3080 | tf_op jit(solution)/shard_map/ppermute | solution.py:21
  351.3 13.0 %collective-permute-start.23 = (f32[1,256]{1,0:T(1,128)S(1)}, f32[1,256]{1,0:T(1,128)S(1)}, u32[]{:S(2)}, u32[]{:S(2)}) collective-permute-start(f32[1,256]{1,0:T(1,128)S(1)} %get-tuple-element.160), channel_id=1, source_target_pairs={{0,8},{8,16},{16,24},{24,32},{32,40},{40,48},{48,56},{56,64},{64,7... | collective-permute-start | bytes 3080 | tf_op jit(solution)/shard_map/ppermute | solution.py:21
  368.5 52.9 %all-to-all-start.3 = ((f32[128,1,2]{2,1,0:T(1,128)}), f32[128,1,2]{2,1,0:T(1,128)}, u32[]{:S(2)}, u32[]{:S(2)}) async-start(f32[128,1,2]{2,1,0:T(1,128)} %broadcast_in_dim.62), calls=%async_computation.3 | async-start | bytes 131072 | tf_op jit(solution)/shard_map/all_to_all | solution.py:141
  427.5 27.0 %collective-permute-start.26 = (f32[1,256]{1,0:T(1,128)}, f32[1,256]{1,0:T(1,128)}, u32[]{:S(2)}, u32[]{:S(2)}) collective-permute-start(f32[1,256]{1,0:T(1,128)} %get-tuple-element.158), channel_id=1, source_target_pairs={{8,0},{16,8},{24,16},{32,24},{40,32},{48,40},{56,48},{64,56},{72,6... | collective-permute-start | bytes 3080 | tf_op jit(solution)/shard_map/ppermute | solution.py:22
  428.8 20.3 %collective-permute-start.27 = (f32[1,256]{1,0:T(1,128)}, f32[1,256]{1,0:T(1,128)}, u32[]{:S(2)}, u32[]{:S(2)}) collective-permute-start(f32[1,256]{1,0:T(1,128)} %get-tuple-element.159), channel_id=1, source_target_pairs={{0,8},{8,16},{16,24},{24,32},{32,40},{40,48},{48,56},{56,64},{64,7... | collective-permute-start | bytes 3080 | tf_op jit(solution)/shard_map/ppermute | solution.py:21
  461.9 13.4 %collective-permute-start.31 = (f32[1,128]{1,0:T(1,128)S(1)}, f32[1,128]{1,0:T(1,128)S(1)}, u32[]{:S(2)}, u32[]{:S(2)}) collective-permute-start(f32[1,128]{1,0:T(1,128)S(1)} %get-tuple-element.208), channel_id=1, source_target_pairs={{0,8},{8,16},{16,24},{24,32},{32,40},{40,48},{48,56},{56,64},{64,7... | collective-permute-start | bytes 1544 | tf_op jit(solution)/shard_map/ppermute | solution.py:21
  583.9 14.4 %collective-permute-start.39 = (f32[1,256]{1,0:T(1,128)}, f32[1,256]{1,0:T(1,128)}, u32[]{:S(2)}, u32[]{:S(2)}) collective-permute-start(f32[1,256]{1,0:T(1,128)} %get-tuple-element.144), channel_id=1, source_target_pairs={{0,8},{8,16},{16,24},{24,32},{32,40},{40,48},{48,56},{56,64},{64,7... | collective-permute-start | bytes 3080 | tf_op jit(solution)/shard_map/ppermute | solution.py:21
  601.8 26.2 %all-to-all-start.5 = ((f32[128,1,1]{2,1,0:T(1,128)}), f32[128,1,1]{2,1,0:T(1,128)}, u32[]{:S(2)}, u32[]{:S(2)}) async-start(f32[128,1,1]{2,1,0:T(1,128)} %broadcast_in_dim.69), calls=%async_computation.5 | async-start | bytes 131072 | tf_op jit(solution)/shard_map/all_to_all | solution.py:141
  631.8 13.3 %collective-permute-start.43 = (f32[1,256]{1,0:T(1,128)S(1)}, f32[1,256]{1,0:T(1,128)S(1)}, u32[]{:S(2)}, u32[]{:S(2)}) collective-permute-start(f32[1,256]{1,0:T(1,128)S(1)} %get-tuple-element.136), channel_id=1, source_target_pairs={{0,8},{8,16},{16,24},{24,32},{32,40},{40,48},{48,56},{56,64},{64,7... | collective-permute-start | bytes 3080 | tf_op jit(solution)/shard_map/ppermute | solution.py:21
  648.6 27.0 %all-to-all-start.6 = ((f32[128,1,1]{2,1,0:T(1,128)}), f32[128,1,1]{2,1,0:T(1,128)}, u32[]{:S(2)}, u32[]{:S(2)}) async-start(f32[128,1,1]{2,1,0:T(1,128)} %broadcast_in_dim.71), calls=%async_computation.6 | async-start | bytes 131072 | tf_op jit(solution)/shard_map/all_to_all | solution.py:141
  681.5 26.9 %collective-permute-start.46 = (f32[1,256]{1,0:T(1,128)}, f32[1,256]{1,0:T(1,128)}, u32[]{:S(2)}, u32[]{:S(2)}) collective-permute-start(f32[1,256]{1,0:T(1,128)} %get-tuple-element.134), channel_id=1, source_target_pairs={{8,0},{16,8},{24,16},{32,24},{40,32},{48,40},{56,48},{64,56},{72,6... | collective-permute-start | bytes 3080 | tf_op jit(solution)/shard_map/ppermute | solution.py:22
  682.8 20.2 %collective-permute-start.47 = (f32[1,256]{1,0:T(1,128)}, f32[1,256]{1,0:T(1,128)}, u32[]{:S(2)}, u32[]{:S(2)}) collective-permute-start(f32[1,256]{1,0:T(1,128)} %get-tuple-element.135), channel_id=1, source_target_pairs={{0,8},{8,16},{16,24},{24,32},{32,40},{40,48},{48,56},{56,64},{64,7... | collective-permute-start | bytes 3080 | tf_op jit(solution)/shard_map/ppermute | solution.py:21
  716.0 13.4 %collective-permute-start.51 = (f32[1,128]{1,0:T(1,128)S(1)}, f32[1,128]{1,0:T(1,128)S(1)}, u32[]{:S(2)}, u32[]{:S(2)}) collective-permute-start(f32[1,128]{1,0:T(1,128)S(1)} %get-tuple-element.192), channel_id=1, source_target_pairs={{0,8},{8,16},{16,24},{24,32},{32,40},{40,48},{48,56},{56,64},{64,7... | collective-permute-start | bytes 1544 | tf_op jit(solution)/shard_map/ppermute | solution.py:21
  849.0 19.4 %all-to-all-start.8 = ((f32[128,1,1]{2,1,0:T(1,128)}), f32[128,1,1]{2,1,0:T(1,128)S(1)}, u32[]{:S(2)}, u32[]{:S(2)}) async-start(f32[128,1,1]{2,1,0:T(1,128)} %broadcast_in_dim.78), calls=%async_computation.8 | async-start | bytes 131072 | tf_op jit(solution)/shard_map/all_to_all | solution.py:141
  (144 other events, 2042.6 us)
